TPU v7x, 256 devices: a whole 4x4x8 slice. The times are simulated.
256 devices in a mesh: req: 64 (over z, x, core), tp: 4 (over y).
Axes of the slice: x: 4, y: 4, z: 8, core: 2. Of those that a mesh axis runs over, the one named last changes fastest.
Arguments:
- hidden: bfloat16 [16384, 2048], P('req'), may hold values from -10.5 to 10.5
- lengths: int32 [64], replicated, may hold values from 1 to 1024, 16384 in all
- dealing: int32 [64], replicated, may hold values from 0 to 63, each once
- norm_gain: bfloat16 [2048], replicated, may hold values from 0.5 to 1.5
- w_query: bfloat16 [2048, 2048], P(None, 'tp'), may hold values from -0.125 to 0.125
- w_key: bfloat16 [2048, 1024], P(None, 'tp'), may hold values from -0.125 to 0.125
- w_value: bfloat16 [2048, 1024], P(None, 'tp'), may hold values from -0.125 to 0.125
- query_gain: bfloat16 [128], replicated, may hold values from 0.5 to 8
- key_gain: bfloat16 [128], replicated, may hold values from 0.5 to 8
- w_out: bfloat16 [2048, 2048], P(None, 'tp'), may hold values from -0.125 to 0.125
Outputs:
- hidden_out: bfloat16 [16384, 2048], P('req', 'tp')
- kv_cache: bfloat16 [2, 64, 1024, 1024], P(None, 'req', None, 'tp')
Inputs may be any that keep to these rules, and one draw needn't show every extreme that they name: The lengths sum to 16384; the largest is exactly 1024. A permutation: dealt slot j, on device j of req, holds prompt dealing[j].
All inputs are finite; a program needn't handle non-finite values.
Results may differ from a plain program's by a relative error of at most 0.012.
The roundings to bfloat16 on the way count: a program that leaves them out, or rounds other values in their place, can miss the bound.
Values may be sent and summed in bfloat16 or wider, within the bound.
No kernel may reach another device: no remote copies, remote signals or barrier semaphores. Data moves between devices by JAX's collectives and lax.ppermute only.
A program may use at most 128 MiB of HBM per device.

v0:
```python
import jax
import jax.numpy as jnp
from jax import lax
from jax.sharding import PartitionSpec as P

EPS = 1e-06
THETA = 1000000.0


def rms_rows(values, scale_gain):
    inv_rms = lax.rsqrt(jnp.mean(values * values, axis=-1, keepdims=True) + EPS)
    return values * inv_rms * scale_gain


def rotate(values, positions):
    features = values.shape[-1]
    half_width = features // 2
    frequency = THETA ** (-(jnp.arange(half_width).astype(jnp.float32) * 2.0) / features)
    angles = positions.astype(jnp.float32)[:, None] * frequency[None, :]
    cosine = jnp.cos(angles)[:, None, :]
    sine_part = jnp.sin(angles)[:, None, :]
    first_half = values[..., :half_width]
    second_half = values[..., half_width:]
    return jnp.concatenate(
        [
            first_half * cosine - second_half * sine_part,
            second_half * cosine + first_half * sine_part,
        ],
        axis=-1,
    )


def project(normed, w_query, w_key, w_value, query_gain, key_gain, positions):
    head_dim = query_gain.shape[0]
    row_count = normed.shape[0]
    query_rows = jnp.dot(normed, w_query, preferred_element_type=jnp.float32).reshape(
        row_count, -1, head_dim
    )
    key_rows = jnp.dot(normed, w_key, preferred_element_type=jnp.float32).reshape(
        row_count, -1, head_dim
    )
    value_rows = jnp.dot(normed, w_value, preferred_element_type=jnp.float32).astype(jnp.bfloat16)
    query_rows = rotate(rms_rows(query_rows, query_gain.astype(jnp.float32)), positions).astype(
        jnp.bfloat16
    )
    key_rows = rotate(rms_rows(key_rows, key_gain.astype(jnp.float32)), positions).astype(
        jnp.bfloat16
    )
    return (query_rows.reshape(row_count, -1), key_rows.reshape(row_count, -1), value_rows)


def attend(query_slot, key_slot, value_slot, prompt_length, head_dim):
    slot_len, query_width = query_slot.shape
    kv_heads = key_slot.shape[1] // head_dim
    group_size = query_width // head_dim // kv_heads
    queries = query_slot.reshape(slot_len, kv_heads, group_size, head_dim)
    keys_split = key_slot.reshape(slot_len, kv_heads, head_dim)
    values_split = value_slot.reshape(slot_len, kv_heads, head_dim)
    scores = jnp.einsum(
        "qkgd,skd->kgqs", queries, keys_split, preferred_element_type=jnp.float32
    ) * head_dim ** (-0.5)
    offsets = jnp.arange(slot_len, dtype=jnp.int32)
    allowed = (offsets[None, :] <= offsets[:, None]) & (offsets[None, :] < prompt_length)
    scores = jnp.where(allowed[None, None], scores, -jnp.inf)
    row_max = jnp.max(scores, axis=-1, keepdims=True)
    weights = jnp.exp(scores - row_max)
    weights = (weights / jnp.sum(weights, axis=-1, keepdims=True)).astype(jnp.bfloat16)
    mixture = jnp.einsum(
        "kgqs,skd->qkgd", weights, values_split, preferred_element_type=jnp.float32
    )
    return mixture.astype(jnp.bfloat16).reshape(slot_len, query_width)


def on_device(
    hidden, lengths, dealing, norm_gain, w_query, w_key, w_value, query_gain, key_gain, w_out
):
    devices = lax.axis_size("req")
    home_index = lax.axis_index("req")
    slice_index = lax.axis_index("tp")
    tok_rows, features = hidden.shape
    head_dim = query_gain.shape[0]
    out_width = w_out.shape[1]
    slot_len = 4 * tok_rows
    capacity = slot_len // devices
    prompt_total = lengths.shape[0]
    prompt_ids = jnp.arange(prompt_total, dtype=jnp.int32)
    prompt_ends = jnp.cumsum(lengths)
    starts = prompt_ends - lengths
    packed_ids = jnp.arange(tok_rows, dtype=jnp.int32) * devices + home_index
    segment = jnp.sum((packed_ids[:, None] >= prompt_ends[None, :]).astype(jnp.int32), axis=1)
    seg_onehot = (segment[:, None] == prompt_ids[None, :]).astype(jnp.int32)
    positions = packed_ids - jnp.sum(seg_onehot * starts[None, :], axis=1)
    inverse = jnp.zeros((prompt_total,), jnp.int32).at[dealing].set(prompt_ids)
    deal_hot = (dealing[:, None] == prompt_ids[None, :]).astype(jnp.int32)
    dealt_starts = jnp.sum(deal_hot * starts[None, :], axis=1)
    dealt_lengths = jnp.sum(deal_hot * lengths[None, :], axis=1)
    first_offset = jnp.mod(home_index - dealt_starts, devices)
    ranks = jnp.arange(capacity, dtype=jnp.int32)
    slot_offset = first_offset[None, :] + ranks[:, None] * devices
    send_valid = slot_offset < dealt_lengths[None, :]
    send_rows = jnp.where(
        send_valid, (dealt_starts[None, :] + slot_offset - home_index) // devices, 0
    ).reshape(-1)
    my_start = lax.dynamic_index_in_dim(dealt_starts, home_index, 0, keepdims=False)
    my_length = lax.dynamic_index_in_dim(dealt_lengths, home_index, 0, keepdims=False)
    roll_shift = jnp.mod(my_start, devices)
    my_slots = jnp.sum(seg_onehot * inverse[None, :], axis=1)
    back_rows = positions // devices * devices + my_slots
    offsets = jnp.arange(slot_len, dtype=jnp.int32)
    gain_values = norm_gain.astype(jnp.float32)
    picked = jnp.take(hidden, send_rows, axis=0).reshape(capacity, devices, hidden.shape[1])
    arrived = lax.all_to_all(
        jnp.where(send_valid[:, :, None], picked, jnp.zeros((), hidden.dtype)),
        "req",
        split_axis=1,
        concat_axis=1,
        tiled=True,
    )
    slot_hidden = jnp.roll(arrived, -roll_shift, axis=1).reshape(slot_len, arrived.shape[2])
    normed = rms_rows(slot_hidden.astype(jnp.float32), gain_values).astype(jnp.bfloat16)
    query_slot, key_slot, value_slot = project(
        normed, w_query, w_key, w_value, query_gain, key_gain, offsets
    )
    mixture = attend(query_slot, key_slot, value_slot, my_length, head_dim)
    sendback = jnp.roll(mixture.reshape(capacity, devices, mixture.shape[1]), roll_shift, axis=1)
    returned = lax.all_to_all(sendback, "req", split_axis=1, concat_axis=1, tiled=True)
    attended = jnp.take(returned.reshape(capacity * devices, -1), back_rows, axis=0)
    kv_cache = jnp.stack([key_slot, value_slot])[:, None]
    summed = jnp.dot(
        lax.all_gather(attended, "tp", axis=1, tiled=True),
        w_out,
        preferred_element_type=jnp.float32,
    )
    branch = lax.optimization_barrier(summed.astype(jnp.bfloat16))
    residual = lax.dynamic_slice_in_dim(hidden, slice_index * out_width, out_width, 1)
    hidden_out = (residual.astype(jnp.float32) + branch.astype(jnp.float32)).astype(jnp.bfloat16)
    return (hidden_out, kv_cache)


def solution(mesh):
    in_specs = (
        P("req", None),
        P(),
        P(),
        P(),
        P(None, "tp"),
        P(None, "tp"),
        P(None, "tp"),
        P(),
        P(),
        P(None, "tp"),
    )
    out_specs = (P("req", "tp"), P(None, "req", None, "tp"))
    return jax.shard_map(
        on_device, mesh=mesh, in_specs=in_specs, out_specs=out_specs, check_vma=False
    )
```

profile of v0, /device:TPU:2, one launch (start us, length us, event | category | flops | bytes accessed | tf_op | source)
XLA Modules:
  0.0 272.4 jit_solution(343829114084428690)
XLA Ops:
  11.1 10.2 %gather_fusion = bf16[1024,2048]{1,0:T(8,128)(2,1)} fusion(bf16[256,2048]{1,0:T(8,128)(2,1)} %param.10, s32[1024]{0:T(1024)S(1)} %broadcast_clamp_fusion), kind=kCustom, calls=%fused_computation | custom fusion | bytes 8392704 | tf_op jit(solution)/shard_map/jit(_take)/gather | solution.py:111
  21.3 9.6 %fusion.10 = bf16[16,64,2048]{2,0,1:T(8,128)(2,1)} fusion(bf16[16,64,2048]{2,1,0:T(8,128)(2,1)} %bitcast.70, pred[16,64]{0,1:T(8,128)(4,1)S(1)} %copy.60, pred[16,64]{0,1:T(8,128)(4,1)S(1)} %copy.59), kind=kLoop, calls=%fused_computation.22 | loop fusion | flops 4194304 | bytes 8390656 | tf_op jit(solution)/shard_map/jit(_where)/select_n | solution.py:113
  30.9 12.3 %all-to-all-start = ((bf16[16,64,2048]{2,0,1:T(8,128)(2,1)}), bf16[16,64,2048]{2,0,1:T(8,128)(2,1)}, u32[]{:S(2)}, u32[]{:S(2)}) async-start(bf16[16,64,2048]{2,0,1:T(8,128)(2,1)} %fusion.10), calls=%async_computation | async-start | bytes 8388608 | tf_op jit(solution)/shard_map/all_to_all | solution.py:112
  46.4 4.0 %copy.80 = bf16[512,2048]{1,0:T(8,128)(2,1)} copy(bf16[512,2048]{0,1:T(8,128)(2,1)} %bitcast.76) | data formatting | bytes 4194304 | tf_op jit(solution)/shard_map/dot_general | solution.py:36
  50.4 1.4 copy.77
  53.5 1.3 fusion.11
  54.9 84.4 %all-to-all-done = bf16[16,64,2048]{2,0,1:T(8,128)(2,1)} async-done(((bf16[16,64,2048]{2,0,1:T(8,128)(2,1)}), bf16[16,64,2048]{2,0,1:T(8,128)(2,1)}, u32[]{:S(2)}, u32[]{:S(2)}) %all-to-all-start) | async-done | bytes 4194336 | tf_op jit(solution)/shard_map/all_to_all | solution.py:112
  139.3 4.5 %copy.62 = bf16[16,64,2048]{2,1,0:T(8,128)(2,1)S(1)} copy(bf16[16,64,2048]{2,0,1:T(8,128)(2,1)} %all-to-all-done) | data formatting | bytes 8388608 | tf_op jit(solution)/shard_map/all_to_all | solution.py:112
  143.8 6.5 %multiply_reduce_fusion = (f32[16,64]{1,0:T(8,128)S(1)}, f32[16,64,2048]{2,1,0:T(8,128)}) fusion(s32[]{:T(128)S(6)} %select_n.166, bf16[16,64,2048]{2,1,0:T(8,128)(2,1)S(1)} %copy.62), kind=kLoop, calls=%fused_computation.16 | loop fusion | flops 12581888 | bytes 12587012 | tf_op jit(solution)/shard_map/reduce_sum | solution.py:11
  150.3 4.3 %multiply_convert_fusion = bf16[16,64,2048]{2,1,0:T(8,128)(2,1)S(1)} fusion(f32[16,64,2048]{2,1,0:T(8,128)} %get-tuple-element.17, f32[2048]{0:T(1024)S(1)} %convert_element_type.122, f32[16,64]{1,0:T(8,128)S(1)} %add_rsqrt_fusion.2), kind=kLoop, calls=%fused_computation.15 | loop fusion | flops 6291456 | bytes 12595200 | tf_op jit(solution)/shard_map/convert_element_type | solution.py:120
  154.6 1.5 copy-done.1
  156.1 2.7 fusion.3
  159.5 2.4 multiply_reduce_fusion.1
  162.4 1.2 subtract_convert_fusion
  163.6 2.4 copy.67
  166.0 1.4 copy.66
  167.4 3.9 %multiply_reduce_fusion.2 = (f32[1024,2]{0,1:T(2,128)S(1)}, f32[1024,2,128]{0,2,1:T(8,128)S(1)}) fusion(bf16[1024,2048,1]{1,0,2:T(8,128)(2,1)} %bitcast.73, bf16[2,128,2048]{2,1,0:T(8,128)(2,1)} %bitcast.80), kind=kOutput, calls=%fused_computation.41 | convolution fusion | flops 1074264064 | bytes 6299648 | tf_op jit(solution)/shard_map/dot_general | solution.py:39
  172.4 1.2 copy-done.2
  173.6 2.1 convolution_convert_fusion
  175.7 11.5 %fusion.38 = (f32[2,2,1024]{2,1,0:T(2,128)S(1)}, f32[2,2,1024,1024]{2,3,1,0:T(8,128)}) fusion(pred[1024,1024]{0,1:T(8,128)(4,1)S(1)} %copy-done.5, bf16[1024,2,2,64]{3,0,2,1:T(8,128)(2,1)} %copy.67, bf16[1024,2,2,64]{3,0,2,1:T(8,128)(2,1)} %copy.66, bf16[1024,2,64]{0,2,1:T(8,128)(2,1)} %get-tuple-element.21, bf16[1024,2,64]{0,2,1:T(8,128)(2,1)S(1)} %get-tuple-element.20), kind=kOutput, calls=%fused_computation.108 | convolution fusion | flops 1093665792 | bytes 19415040 | tf_op jit(solution)/shard_map/sub | solution.py:66
  187.1 7.2 %fusion.15 = bf16[1024,2,2,128]{0,3,2,1:T(8,128)(2,1)S(1)} fusion(bf16[1024,2,128,1]{0,2,3,1:T(8,128)(2,1)} %bitcast.81, f32[2,2,1024,1024]{2,3,1,0:T(8,128)} %get-tuple-element.31, f32[2,2,1024]{2,1,0:T(2,128)S(1)} %get-tuple-element.30), kind=kOutput, calls=%fused_computation.31 | convolution fusion | flops 1082654720 | bytes 18366464 | tf_op jit(solution)/shard_map/kgqs,skd->qkgd/dot_general | solution.py:68
  194.4 2.0 copy.70
  196.4 1.5 reshape_reshape.4
  198.7 1.5 copy.71
  200.3 5.6 %all-to-all-start.1 = ((bf16[16,64,512]{2,0,1:T(8,128)(2,1)}), bf16[16,64,512]{2,0,1:T(8,128)(2,1)}, u32[]{:S(2)}, u32[]{:S(2)}) async-start(bf16[16,64,512]{2,0,1:T(8,128)(2,1)} %copy.71), calls=%async_computation.1 | async-start | bytes 2097152 | tf_op jit(solution)/shard_map/all_to_all | solution.py:126
  207.0 27.6 %all-to-all-done.1 = bf16[16,64,512]{2,0,1:T(8,128)(2,1)} async-done(((bf16[16,64,512]{2,0,1:T(8,128)(2,1)}), bf16[16,64,512]{2,0,1:T(8,128)(2,1)}, u32[]{:S(2)}, u32[]{:S(2)}) %all-to-all-start.1) | async-done | bytes 1048608 | tf_op jit(solution)/shard_map/all_to_all | solution.py:126
  234.6 1.8 copy.72
  236.5 1.2 gather_fusion.1
  240.7 1.3 copy.73
  242.0 20.0 %all-gather.2.cloned.1.call-done = bf16[256,2048]{1,0:T(8,128)(2,1)} async-done(((bf16[256,512]{1,0:T(8,128)(2,1)}), bf16[256,2048]{1,0:T(8,128)(2,1)}) %all-gather.2.cloned.1.call-update) | async-done | bytes 1048592 | tf_op jit(solution)/shard_map/all_gather | solution.py:130
  261.9 1.9 convolution_convert_fusion.1
  263.9 1.7 add_convert_fusion.1
  (67 shorter events, 14.0 us)
Async XLA Ops:
  7.2 254.8 %copy-start = (bf16[2048,512]{1,0:T(8,128)(2,1)S(1)}, bf16[2048,512]{1,0:T(8,128)(2,1)}, u32[]{:S(2)}) copy-start(bf16[2048,512]{1,0:T(8,128)(2,1)} %param.19) | copy-start | bytes 6291460
  30.9 15.6 %copy-start.8 = (bf16[2048]{0:T(1024)(128)(2,1)S(1)}, bf16[2048]{0:T(1024)(128)(2,1)}, u32[]{:S(2)}) copy-start(bf16[2048]{0:T(1024)(128)(2,1)} %param.13) | copy-start | bytes 12292
  30.9 108.4 %all-to-all-start = ((bf16[16,64,2048]{2,0,1:T(8,128)(2,1)}), bf16[16,64,2048]{2,0,1:T(8,128)(2,1)}, u32[]{:S(2)}, u32[]{:S(2)}) async-start(bf16[16,64,2048]{2,0,1:T(8,128)(2,1)} %fusion.10), calls=%async_computation | async-start | bytes 8388608 | tf_op jit(solution)/shard_map/all_to_all | solution.py:112
  43.2 7.2 %copy-start.10 = (bf16[128]{0:T(256)(128)(2,1)S(1)}, bf16[128]{0:T(256)(128)(2,1)}, u32[]{:S(2)}) copy-start(bf16[128]{0:T(256)(128)(2,1)} %param.17) | copy-start | bytes 772
  43.2 7.2 %copy-start.6 = (bf16[2048,256]{1,0:T(8,128)(2,1)S(1)}, bf16[2048,256]{1,0:T(8,128)(2,1)}, u32[]{:S(2)}) copy-start(bf16[2048,256]{1,0:T(8,128)(2,1)} %param.15) | copy-start | bytes 3145732
  43.2 8.6 %copy-start.11 = (bf16[128]{0:T(256)(128)(2,1)S(1)}, bf16[128]{0:T(256)(128)(2,1)}, u32[]{:S(2)}) copy-start(bf16[128]{0:T(256)(128)(2,1)} %param.18) | copy-start | bytes 772
  150.3 5.8 %copy-start.1 = (f32[16,64,2048]{2,1,0:T(8,128)S(1)}, f32[16,64,2048]{2,1,0:T(8,128)}, u32[]{:S(2)}) copy-start(f32[16,64,2048]{2,1,0:T(8,128)} %get-tuple-element.17) | copy-start | bytes 25165828
  156.1 3.4 %copy-start.3 = (bf16[16,64,2048]{2,1,0:T(8,128)(2,1)}, bf16[16,64,2048]{2,1,0:T(8,128)(2,1)S(1)}, u32[]{:S(2)}) copy-start(bf16[16,64,2048]{2,1,0:T(8,128)(2,1)S(1)} %multiply_convert_fusion) | copy-start | bytes 12582916
  156.1 3.4 %copy-start.4 = (bf16[512,2048]{1,0:T(8,128)(2,1)S(1)}, bf16[512,2048]{1,0:T(8,128)(2,1)}, u32[]{:S(2)}) copy-start(bf16[512,2048]{1,0:T(8,128)(2,1)} %copy.80) | copy-start | bytes 6291460
  167.4 5.0 %copy-start.9 = (bf16[2048,256]{1,0:T(8,128)(2,1)S(1)}, bf16[2048,256]{1,0:T(8,128)(2,1)}, u32[]{:S(2)}) copy-start(bf16[2048,256]{1,0:T(8,128)(2,1)} %param.16) | copy-start | bytes 3145732
  171.3 2.3 copy-start.2
  173.6 2.1 copy-start.7
  173.6 2.1 copy-start.5
  200.3 34.4 %all-to-all-start.1 = ((bf16[16,64,512]{2,0,1:T(8,128)(2,1)}), bf16[16,64,512]{2,0,1:T(8,128)(2,1)}, u32[]{:S(2)}, u32[]{:S(2)}) async-start(bf16[16,64,512]{2,0,1:T(8,128)(2,1)} %copy.71), calls=%async_computation.1 | async-start | bytes 2097152 | tf_op jit(solution)/shard_map/all_to_all | solution.py:126
  205.9 56.0 %all-gather.2.cloned.1.call-start = ((), (), s32[]{:S(2)}) async-start(), calls=%async_computation.2 | async-start | bytes 1310720 | tf_op jit(solution)/shard_map/all_gather | solution.py:130
Sparse Core Ops, SparseCore 0:
  238.6 23.3 all-gather.1
where the time goes:
time: 273 us; the launch traced here: 272 us
  waiting for transfers between devices  132 us (48%)
  local copies, waits for them, and re-layouts  39.9 us (15%)
  other arithmetic  37.2 us (14%)
  matrix products  29 us (11%)
  starting transfers between devices  18 us (7%)
  between operations  16.3 us (6%)
    all_to_all x1, waiting for transfers between devices, on_device(): lax.all_to_all(jnp.where(send_valid[:, :, None], picked, jnp.zeros((), hi...  84.4 us
    all_to_all x1, waiting for transfers between devices, on_device(): lax.all_to_all(sendback, 'req', split_axis=1, concat_axis=1, tiled=True)  27.6 us
    all_gather x1, waiting for transfers between devices, on_device(): lax.all_gather(attended, 'tp', axis=1, tiled=True)  20 us
    all_to_all x1, starting transfers between devices, on_device(): lax.all_to_all(jnp.where(send_valid[:, :, None], picked, jnp.zeros((), hi...  12.3 us
    sub x1, matrix products, attend(): weights = jnp.exp(scores - row_max)  11.5 us
    gather x1, local copies, waits for them, and re-layouts, on_device(): jnp.take(hidden, send_rows, axis=0)  10.2 us
    select_n x1, other arithmetic, on_device(): jnp.where(send_valid[:, :, None], picked, jnp.zeros((), hidden.dtype))  9.61 us
    dot_general x1, matrix products, attend(): jnp.einsum('kgqs,skd->qkgd', weights, values_split, preferred_element_typ...  7.24 us
  transfers between devices with their start and end apart: 3, of which 3 were waited for; matrix products, arithmetic and copies ran while one was open for 5% of the time, Pallas kernels for 0%

commit v1 on v0

--- a/solution.py
+++ b/solution.py
@@ -127,7 +127,9 @@
     attended = jnp.take(returned.reshape(capacity * devices, -1), back_rows, axis=0)
     kv_cache = jnp.stack([key_slot, value_slot])[:, None]
     summed = jnp.dot(
-        lax.all_gather(attended, "tp", axis=1, tiled=True),
+        jnp.concatenate(
+            lax.all_to_all(jnp.stack([attended] * lax.axis_size("tp")), "tp", 0, 0), axis=1
+        ),
         w_out,
         preferred_element_type=jnp.float32,
     )

time: 273 us -> 256 us (0.938)
  between operations: 16.3 us -> 2.92 us
  waiting for transfers between devices: 132 us -> 124 us
  starting transfers between devices: 18 us -> 22.4 us
    all_gather x1 -> x0, waiting for transfers between devices: 20 us -> none  [on_device(): lax.all_gather(attended, 'tp', axis=1, tiled=True)]
    all_to_all x0 -> x1, waiting for transfers between devices: none -> 11.8 us  [on_device(): lax.all_to_all(jnp.stack([attended] * lax.axis_size('tp')), 'tp', 0, 0)]
    all_to_all x0 -> x1, starting transfers between devices: none -> 4.46 us  [on_device(): lax.all_to_all(jnp.stack([attended] * lax.axis_size('tp')), 'tp', 0, 0)]
where the time goes in v1:
time: 256 us; the launch traced here: 255 us
  waiting for transfers between devices  124 us (48%)
  local copies, waits for them, and re-layouts  41.1 us (16%)
  other arithmetic  35.5 us (14%)
  matrix products  29 us (11%)
  starting transfers between devices  22.4 us (9%)
  between operations  2.92 us (1%)
    all_to_all x1, waiting for transfers between devices, on_device(): lax.all_to_all(jnp.where(send_valid[:, :, None], picked, jnp.zeros((), hi...  84.4 us
    all_to_all x1, waiting for transfers between devices, on_device(): lax.all_to_all(sendback, 'req', split_axis=1, concat_axis=1, tiled=True)  27.7 us
    all_to_all x1, starting transfers between devices, on_device(): lax.all_to_all(jnp.where(send_valid[:, :, None], picked, jnp.zeros((), hi...  12.3 us
    all_to_all x1, waiting for transfers between devices, on_device(): lax.all_to_all(jnp.stack([attended] * lax.axis_size('tp')), 'tp', 0, 0)  11.8 us
    sub x1, matrix products, attend(): weights = jnp.exp(scores - row_max)  11.5 us
    gather x1, local copies, waits for them, and re-layouts, on_device(): jnp.take(hidden, send_rows, axis=0)  10.2 us
    select_n x1, other arithmetic, on_device(): jnp.where(send_valid[:, :, None], picked, jnp.zeros((), hidden.dtype))  9.61 us
    dot_general x1, matrix products, attend(): jnp.einsum('kgqs,skd->qkgd', weights, values_split, preferred_element_typ...  7.24 us
  transfers between devices with their start and end apart: 3, of which 3 were waited for; matrix products, arithmetic and copies ran while one was open for 5% of the time, Pallas kernels for 0%

profile of v1, /device:TPU:2, one launch (start us, length us, event | category | flops | bytes accessed | tf_op | source)
XLA Modules:
  0.0 254.9 jit_solution(9027542502763500314)
XLA Ops:
  4.5 10.2 %gather_fusion = bf16[1024,2048]{1,0:T(8,128)(2,1)} fusion(bf16[256,2048]{1,0:T(8,128)(2,1)} %param.10, s32[1024]{0:T(1024)S(1)} %broadcast_clamp_fusion), kind=kCustom, calls=%fused_computation | custom fusion | bytes 8392704 | tf_op jit(solution)/shard_map/jit(_take)/gather | solution.py:111
  14.7 9.6 %fusion.10 = bf16[16,64,2048]{2,0,1:T(8,128)(2,1)} fusion(bf16[16,64,2048]{2,1,0:T(8,128)(2,1)} %bitcast.73, pred[16,64]{0,1:T(8,128)(4,1)S(1)} %copy.63, pred[16,64]{0,1:T(8,128)(4,1)S(1)} %copy.62), kind=kLoop, calls=%fused_computation.22 | loop fusion | flops 4194304 | bytes 8390656 | tf_op jit(solution)/shard_map/jit(_where)/select_n | solution.py:113
  24.3 12.3 %all-to-all-start = ((bf16[16,64,2048]{2,0,1:T(8,128)(2,1)}), bf16[16,64,2048]{2,0,1:T(8,128)(2,1)}, u32[]{:S(2)}, u32[]{:S(2)}) async-start(bf16[16,64,2048]{2,0,1:T(8,128)(2,1)} %fusion.10), calls=%async_computation | async-start | bytes 8388608 | tf_op jit(solution)/shard_map/all_to_all | solution.py:112
  39.9 4.0 %copy.84 = bf16[512,2048]{1,0:T(8,128)(2,1)} copy(bf16[512,2048]{0,1:T(8,128)(2,1)} %bitcast.79) | data formatting | bytes 4194304 | tf_op jit(solution)/shard_map/dot_general | solution.py:36
  43.9 1.4 copy.81
  47.0 1.3 fusion.11
  48.3 84.4 %all-to-all-done = bf16[16,64,2048]{2,0,1:T(8,128)(2,1)} async-done(((bf16[16,64,2048]{2,0,1:T(8,128)(2,1)}), bf16[16,64,2048]{2,0,1:T(8,128)(2,1)}, u32[]{:S(2)}, u32[]{:S(2)}) %all-to-all-start) | async-done | bytes 4194336 | tf_op jit(solution)/shard_map/all_to_all | solution.py:112
  132.8 4.5 %copy.65 = bf16[16,64,2048]{2,1,0:T(8,128)(2,1)S(1)} copy(bf16[16,64,2048]{2,0,1:T(8,128)(2,1)} %all-to-all-done) | data formatting | bytes 8388608 | tf_op jit(solution)/shard_map/all_to_all | solution.py:112
  137.3 6.5 %multiply_reduce_fusion = (f32[16,64]{1,0:T(8,128)S(1)}, f32[16,64,2048]{2,1,0:T(8,128)}) fusion(s32[]{:T(128)S(6)} %select_n.168, bf16[16,64,2048]{2,1,0:T(8,128)(2,1)S(1)} %copy.65), kind=kLoop, calls=%fused_computation.16 | loop fusion | flops 12581888 | bytes 12587012 | tf_op jit(solution)/shard_map/reduce_sum | solution.py:11
  143.8 4.3 %multiply_convert_fusion = bf16[16,64,2048]{2,1,0:T(8,128)(2,1)S(1)} fusion(f32[16,64,2048]{2,1,0:T(8,128)} %get-tuple-element.17, f32[2048]{0:T(1024)S(1)} %convert_element_type.122, f32[16,64]{1,0:T(8,128)S(1)} %add_rsqrt_fusion.2), kind=kLoop, calls=%fused_computation.15 | loop fusion | flops 6291456 | bytes 12595200 | tf_op jit(solution)/shard_map/convert_element_type | solution.py:120
  148.1 1.5 copy-done.1
  149.6 2.7 %fusion.3 = bf16[1024,2048]{1,0:T(8,128)(2,1)} fusion(f32[16,64,2048]{2,1,0:T(8,128)S(1)} %copy-done.1, f32[2048]{0:T(1024)S(1)} %convert_element_type.122, f32[1024]{0:T(1024)S(1)} %rsqrt.29), kind=kLoop, calls=%fused_computation.12 | loop fusion | flops 6291456 | bytes 12595200 | tf_op jit(solution)/shard_map/convert_element_type | solution.py:120
  153.0 2.4 multiply_reduce_fusion.1
  155.9 1.2 subtract_convert_fusion
  157.1 2.4 copy.70
  159.5 1.4 copy.69
  160.9 3.9 %multiply_reduce_fusion.2 = (f32[1024,2]{0,1:T(2,128)S(1)}, f32[1024,2,128]{0,2,1:T(8,128)S(1)}) fusion(bf16[1024,2048,1]{1,0,2:T(8,128)(2,1)} %bitcast.76, bf16[2,128,2048]{2,1,0:T(8,128)(2,1)} %bitcast.83), kind=kOutput, calls=%fused_computation.41 | convolution fusion | flops 1074264064 | bytes 6299648 | tf_op jit(solution)/shard_map/dot_general | solution.py:39
  165.9 1.2 copy-done.2
  167.0 2.1 convolution_convert_fusion
  169.1 11.5 %fusion.38 = (f32[2,2,1024]{2,1,0:T(2,128)S(1)}, f32[2,2,1024,1024]{2,3,1,0:T(8,128)}) fusion(pred[1024,1024]{0,1:T(8,128)(4,1)S(1)} %copy-done.5, bf16[1024,2,2,64]{3,0,2,1:T(8,128)(2,1)} %copy.70, bf16[1024,2,2,64]{3,0,2,1:T(8,128)(2,1)} %copy.69, bf16[1024,2,64]{0,2,1:T(8,128)(2,1)} %get-tuple-element.21, bf16[1024,2,64]{0,2,1:T(8,128)(2,1)S(1)} %get-tuple-element.20), kind=kOutput, calls=%fused_computation.108 | convolution fusion | flops 1093665792 | bytes 19415040 | tf_op jit(solution)/shard_map/sub | solution.py:66
  180.6 7.2 %fusion.15 = bf16[1024,2,2,128]{0,3,2,1:T(8,128)(2,1)S(1)} fusion(bf16[1024,2,128,1]{0,2,3,1:T(8,128)(2,1)} %bitcast.84, f32[2,2,1024,1024]{2,3,1,0:T(8,128)} %get-tuple-element.31, f32[2,2,1024]{2,1,0:T(2,128)S(1)} %get-tuple-element.30), kind=kOutput, calls=%fused_computation.31 | convolution fusion | flops 1082654720 | bytes 18366464 | tf_op jit(solution)/shard_map/kgqs,skd->qkgd/dot_general | solution.py:68
  187.9 2.0 copy.73
  189.9 1.5 reshape_reshape.4
  192.2 1.5 copy.74
  193.7 5.6 %all-to-all-start.1 = ((bf16[16,64,512]{2,0,1:T(8,128)(2,1)}), bf16[16,64,512]{2,0,1:T(8,128)(2,1)}, u32[]{:S(2)}, u32[]{:S(2)}) async-start(bf16[16,64,512]{2,0,1:T(8,128)(2,1)} %copy.74), calls=%async_computation.1 | async-start | bytes 2097152 | tf_op jit(solution)/shard_map/all_to_all | solution.py:126
  200.4 27.7 %all-to-all-done.1 = bf16[16,64,512]{2,0,1:T(8,128)(2,1)} async-done(((bf16[16,64,512]{2,0,1:T(8,128)(2,1)}), bf16[16,64,512]{2,0,1:T(8,128)(2,1)}, u32[]{:S(2)}, u32[]{:S(2)}) %all-to-all-start.1) | async-done | bytes 1048608 | tf_op jit(solution)/shard_map/all_to_all | solution.py:126
  228.1 1.8 copy.75
  232.4 4.5 %all-to-all-start.2 = ((bf16[4,256,512]{1,2,0:T(8,128)(2,1)}), bf16[4,256,512]{1,2,0:T(8,128)(2,1)}, u32[]{:S(2)}, u32[]{:S(2)}) async-start(bf16[4,256,512]{1,2,0:T(8,128)(2,1)} %stack.6), calls=%async_computation.2 | async-start | bytes 2097152 | tf_op jit(solution)/shard_map/all_to_all | solution.py:131
  238.1 1.3 copy.77
  239.4 11.8 %all-to-all-done.2 = bf16[4,256,512]{1,2,0:T(8,128)(2,1)} async-done(((bf16[4,256,512]{1,2,0:T(8,128)(2,1)}), bf16[4,256,512]{1,2,0:T(8,128)(2,1)}, u32[]{:S(2)}, u32[]{:S(2)}) %all-to-all-start.2) | async-done | bytes 1048608 | tf_op jit(solution)/shard_map/all_to_all | solution.py:131
  251.2 1.9 convolution_convert_fusion.1
  253.1 1.7 add_convert_fusion.1
  (72 shorter events, 14.6 us)
Async XLA Ops:
  0.6 250.5 %copy-start = (bf16[2048,512]{1,0:T(8,128)(2,1)S(1)}, bf16[2048,512]{1,0:T(8,128)(2,1)}, u32[]{:S(2)}) copy-start(bf16[2048,512]{1,0:T(8,128)(2,1)} %param.19) | copy-start | bytes 6291460
  24.3 15.6 %copy-start.10 = (bf16[2048]{0:T(1024)(128)(2,1)S(1)}, bf16[2048]{0:T(1024)(128)(2,1)}, u32[]{:S(2)}) copy-start(bf16[2048]{0:T(1024)(128)(2,1)} %param.13) | copy-start | bytes 12292
  24.3 108.4 %all-to-all-start = ((bf16[16,64,2048]{2,0,1:T(8,128)(2,1)}), bf16[16,64,2048]{2,0,1:T(8,128)(2,1)}, u32[]{:S(2)}, u32[]{:S(2)}) async-start(bf16[16,64,2048]{2,0,1:T(8,128)(2,1)} %fusion.10), calls=%async_computation | async-start | bytes 8388608 | tf_op jit(solution)/shard_map/all_to_all | solution.py:112
  36.7 7.2 %copy-start.12 = (bf16[128]{0:T(256)(128)(2,1)S(1)}, bf16[128]{0:T(256)(128)(2,1)}, u32[]{:S(2)}) copy-start(bf16[128]{0:T(256)(128)(2,1)} %param.17) | copy-start | bytes 772
  36.7 7.2 %copy-start.6 = (bf16[2048,256]{1,0:T(8,128)(2,1)S(1)}, bf16[2048,256]{1,0:T(8,128)(2,1)}, u32[]{:S(2)}) copy-start(bf16[2048,256]{1,0:T(8,128)(2,1)} %param.15) | copy-start | bytes 3145732
  36.7 8.6 %copy-start.13 = (bf16[128]{0:T(256)(128)(2,1)S(1)}, bf16[128]{0:T(256)(128)(2,1)}, u32[]{:S(2)}) copy-start(bf16[128]{0:T(256)(128)(2,1)} %param.18) | copy-start | bytes 772
  143.8 5.8 %copy-start.1 = (f32[16,64,2048]{2,1,0:T(8,128)S(1)}, f32[16,64,2048]{2,1,0:T(8,128)}, u32[]{:S(2)}) copy-start(f32[16,64,2048]{2,1,0:T(8,128)} %get-tuple-element.17) | copy-start | bytes 25165828
  149.6 3.4 %copy-start.3 = (bf16[16,64,2048]{2,1,0:T(8,128)(2,1)}, bf16[16,64,2048]{2,1,0:T(8,128)(2,1)S(1)}, u32[]{:S(2)}) copy-start(bf16[16,64,2048]{2,1,0:T(8,128)(2,1)S(1)} %multiply_convert_fusion) | copy-start | bytes 12582916
  149.6 3.4 %copy-start.4 = (bf16[512,2048]{1,0:T(8,128)(2,1)S(1)}, bf16[512,2048]{1,0:T(8,128)(2,1)}, u32[]{:S(2)}) copy-start(bf16[512,2048]{1,0:T(8,128)(2,1)} %copy.84) | copy-start | bytes 6291460
  160.9 5.0 %copy-start.11 = (bf16[2048,256]{1,0:T(8,128)(2,1)S(1)}, bf16[2048,256]{1,0:T(8,128)(2,1)}, u32[]{:S(2)}) copy-start(bf16[2048,256]{1,0:T(8,128)(2,1)} %param.16) | copy-start | bytes 3145732
  164.8 2.3 copy-start.2
  167.0 2.1 copy-start.7
  167.0 2.1 copy-start.5
  193.7 34.4 %all-to-all-start.1 = ((bf16[16,64,512]{2,0,1:T(8,128)(2,1)}), bf16[16,64,512]{2,0,1:T(8,128)(2,1)}, u32[]{:S(2)}, u32[]{:S(2)}) async-start(bf16[16,64,512]{2,0,1:T(8,128)(2,1)} %copy.74), calls=%async_computation.1 | async-start | bytes 2097152 | tf_op jit(solution)/shard_map/all_to_all | solution.py:126
  231.1 5.8 %copy-start.8 = (bf16[1024,2,64]{0,2,1:T(8,128)(2,1)S(1)}, bf16[1024,2,64]{0,2,1:T(8,128)(2,1)}, u32[]{:S(2)}) copy-start(bf16[1024,2,64]{0,2,1:T(8,128)(2,1)} %copy-done.7) | copy-start | bytes 786436
  231.1 5.8 %copy-start.9 = (bf16[1024,2,64]{0,2,1:T(8,128)(2,1)S(1)}, bf16[1024,2,64]{0,2,1:T(8,128)(2,1)}, u32[]{:S(2)}) copy-start(bf16[1024,2,64]{0,2,1:T(8,128)(2,1)} %get-tuple-element.21) | copy-start | bytes 786436
  232.4 18.7 %all-to-all-start.2 = ((bf16[4,256,512]{1,2,0:T(8,128)(2,1)}), bf16[4,256,512]{1,2,0:T(8,128)(2,1)}, u32[]{:S(2)}, u32[]{:S(2)}) async-start(bf16[4,256,512]{1,2,0:T(8,128)(2,1)} %stack.6), calls=%async_computation.2 | async-start | bytes 2097152 | tf_op jit(solution)/shard_map/all_to_all | solution.py:131
